TPU v7x, 512 devices: a whole 4x4x16 slice. The times are simulated.
512 devices in a mesh: dp: 16 (over z), row: 4 (over y), col: 8 (over x, core).
Axes of the slice: x: 4, y: 4, z: 16, core: 2. Of those that a mesh axis runs over, the one named last changes fastest.
Arguments:
- layer_input: bfloat16 [3072, 4096], P(('dp', 'col'), 'row'), may hold values from -6 to 6
- hidden_grad: bfloat16 [3072, 14336], P(('dp', 'row'), 'col'), may hold values from -6 to 6
- gate_slots: bfloat16 [4, 8, 48, 128, 128], P('row', 'col', 'dp'), may hold values from -0.125 to 0.125
- up_slots: bfloat16 [4, 8, 48, 128, 128], P('row', 'col', 'dp'), may hold values from -0.125 to 0.125
- block_mask: int32 [32, 112], replicated, may hold values from 0 to 1, as said below
Outputs:
- input_grad: bfloat16 [3072, 4096], P(('dp', 'col'), 'row')
- gate_slot_grad: float32 [4, 8, 48, 128, 128], P('row', 'col', 'dp')
- up_slot_grad: float32 [4, 8, 48, 128, 128], P('row', 'col', 'dp')
Inputs may be any that keep to these rules, and one draw needn't show every extreme that they name: `block_mask`: every tile of 8 x 14 blocks keeps between 24 and 48 blocks; some tile keeps exactly 48, which tile depends on the draw.
All inputs are finite; a program needn't handle non-finite values.
Results may differ from a plain program's by a relative error of at most 0.022.
Values may be sent and summed in bfloat16 or wider, within the bound.
No kernel may reach another device: no remote copies, remote signals or barrier semaphores. Data moves between devices by JAX's collectives and lax.ppermute only.
A program may use at most 64 MiB of HBM per device.

v0:
```python
import jax
import jax.numpy as jnp
from jax import lax
from jax.sharding import PartitionSpec as P

F32 = jnp.float32
BF16 = jnp.bfloat16


def _shift(x, axis, n, step):
    return lax.ppermute(x, axis, perm=[(i, (i + step) % n) for i in range(n)])


def ring_gather(x, axis, n):
    ahead = n // 2
    behind = n - 1 - ahead
    out = [None] * n
    out[0] = x
    fwd = x
    bwd = x
    for s in range(1, ahead + 1):
        fwd = _shift(fwd, axis, n, 1)
        out[(n - s) % n] = fwd
        if s <= behind:
            bwd = _shift(bwd, axis, n, -1)
            out[s] = bwd
    return out


def ring_sum_scatter(parts, axis, n):
    ahead = n // 2
    behind = n - 1 - ahead
    fwd = parts[ahead]
    bwd = parts[(n - behind) % n] if behind > 0 else None
    for s in range(1, ahead + 1):
        fwd = _shift(fwd, axis, n, 1)
        total = fwd.astype(F32) + parts[ahead - s].astype(F32)
        fwd = total.astype(BF16) if s < ahead else total
        if s <= behind:
            bwd = _shift(bwd, axis, n, -1)
            if s < behind:
                bwd = (bwd.astype(F32) + parts[(s - behind) % n].astype(F32)).astype(BF16)
    if bwd is None:
        return fwd
    return fwd + bwd.astype(F32)


def on_device(layer_input, hidden_grad, gate_slots, up_slots, block_mask):
    n_dp = lax.axis_size("dp")
    n_row = lax.axis_size("row")
    n_col = lax.axis_size("col")
    k_dp = lax.axis_index("dp")
    k_row = lax.axis_index("row")
    k_col = lax.axis_index("col")
    bs = gate_slots.shape[-1]
    per_dev = gate_slots.shape[2]
    cap = per_dev * n_dp
    feat = layer_input.shape[1]
    units = hidden_grad.shape[1]
    tile_rows = feat // bs
    tile_cols = units // bs
    tok = layer_input.shape[0] * n_col
    rows_per = tok // n_row
    cols_per = tok // n_col
    gate_all = lax.all_gather(
        gate_slots[0, 0].reshape(per_dev * bs, bs), "dp", axis=0, tiled=True
    ).reshape(cap, bs, bs)
    up_all = lax.all_gather(
        up_slots[0, 0].reshape(per_dev * bs, bs), "dp", axis=0, tiled=True
    ).reshape(cap, bs, bs)
    x_rel = jnp.stack(ring_gather(layer_input, "col", n_col))
    x_abs = jnp.roll(x_rel, k_col, axis=0).reshape(tok, tile_rows, bs)
    tile_mask = lax.dynamic_slice(
        block_mask, (k_row * tile_rows, k_col * tile_cols), (tile_rows, tile_cols)
    ).reshape(tile_rows * tile_cols)
    kept = tile_mask > 0
    position = jnp.cumsum(kept.astype(jnp.int32)) - 1
    q = jnp.arange(cap, dtype=jnp.int32)
    picks = kept[None, :] & (position[None, :] == q[:, None])
    onehot3 = picks.astype(BF16).reshape(cap, tile_rows, tile_cols)
    row_pick = jnp.sum(onehot3, axis=2)
    col_pick = jnp.sum(onehot3, axis=1)
    high = lax.Precision.HIGH
    x_pick = jnp.einsum("qr,trk->qtk", row_pick, x_abs, preferred_element_type=F32).astype(BF16)

    def pre_rows(weights):
        per_slot = jnp.einsum("qtk,qkn->qtn", x_pick, weights, preferred_element_type=F32)
        pre = jnp.einsum(
            "qc,qtn->ctn",
            col_pick.astype(F32),
            per_slot,
            precision=high,
            preferred_element_type=F32,
        ).astype(BF16)
        pre_roll = jnp.roll(pre.reshape(tile_cols, n_row, rows_per, bs), -k_row, axis=1)
        return ring_sum_scatter([pre_roll[:, m] for m in range(n_row)], "row", n_row)

    gate = pre_rows(gate_all)
    up = pre_rows(up_all)
    upstream = hidden_grad.astype(F32).reshape(rows_per, tile_cols, bs).transpose(1, 0, 2)
    sig = jax.nn.sigmoid(gate)
    gate_grad = (upstream * up * sig * (1.0 + gate * (1.0 - sig))).astype(BF16)
    up_grad = (upstream * gate * sig).astype(BF16)

    def grad_slots(grad_part):
        grad_rel = jnp.stack(ring_gather(grad_part, "row", n_row), axis=1)
        grad_abs = jnp.roll(grad_rel, k_row, axis=1).reshape(tile_cols, tok, bs)
        return jnp.einsum("qc,ctn->qtn", col_pick, grad_abs, preferred_element_type=F32).astype(
            BF16
        )

    def slot_grad(picked):
        slot_dw = jnp.einsum("qtk,qtn->qkn", x_pick, picked, preferred_element_type=F32).astype(
            BF16
        )
        total = lax.psum_scatter(
            slot_dw.reshape(cap * bs, bs), "dp", scatter_dimension=0, tiled=True
        )
        return (total.astype(F32) / n_dp).reshape(per_dev, bs, bs)[None, None]

    gate_pick = grad_slots(gate_grad)
    gate_out = slot_grad(gate_pick)
    up_pick = grad_slots(up_grad)
    up_out = slot_grad(up_pick)
    dx_slot = jnp.einsum("qtn,qkn->qtk", gate_pick, gate_all, preferred_element_type=F32)
    dx_slot = dx_slot + jnp.einsum("qtn,qkn->qtk", up_pick, up_all, preferred_element_type=F32)
    dx = jnp.einsum(
        "qr,qtk->rtk", row_pick.astype(F32), dx_slot, precision=high, preferred_element_type=F32
    ).astype(BF16)
    dx_roll = jnp.roll(dx.reshape(tile_rows, n_col, cols_per, bs), -k_col, axis=1)
    dx_sum = ring_sum_scatter([dx_roll[:, m] for m in range(n_col)], "col", n_col)
    input_grad = dx_sum.transpose(1, 0, 2).reshape(cols_per, feat).astype(BF16)
    return (input_grad, gate_out, up_out)


def solution(mesh):
    return jax.shard_map(
        on_device,
        mesh=mesh,
        in_specs=(
            P(("dp", "col"), "row"),
            P(("dp", "row"), "col"),
            P("row", "col", "dp", None, None),
            P("row", "col", "dp", None, None),
            P(),
        ),
        out_specs=(
            P(("dp", "col"), "row"),
            P("row", "col", "dp", None, None),
            P("row", "col", "dp", None, None),
        ),
        check_vma=False,
    )
```

profile of v0, /device:TPU:2, one launch (start us, length us, event | category | flops | bytes accessed | tf_op | source)
XLA Modules:
  0.0 373.9 jit_solution(405065625400467713)
XLA Ops:
  11.1 5.3 %collective-permute-start.1 = (bf16[24,1024]{1,0:T(8,128)(2,1)S(1)}, bf16[24,1024]{1,0:T(8,128)(2,1)S(1)}, u32[]{:S(2)}, u32[]{:S(2)}) collective-permute-start(bf16[24,1024]{1,0:T(8,128)(2,1)S(1)} %collective-permute-done), channel_id=1, source_target_pairs={{0,7},{1,0},{2,1},{3,2},{4,3},{5,4},{6,5},{7,6},{8,15},{9,8},{10,9... | collective-permute-start | bytes 147464 | tf_op jit(solution)/shard_map/ppermute | solution.py:11
  16.5 1.7 collective-permute-done.1
  18.2 1.8 collective-permute-start.2
  20.0 3.5 collective-permute-done.5
  23.5 3.5 collective-permute-done.6
  28.9 57.6 %all-gather.3.cloned.1.call-done = bf16[6144,128]{1,0:T(8,128)(2,1)} async-done(((bf16[384,128]{1,0:T(8,128)(2,1)}), bf16[6144,128]{1,0:T(8,128)(2,1)}) %all-gather.3.cloned.1.call-update) | async-done | bytes 1572880 | tf_op jit(solution)/shard_map/all_gather | solution.py:68
  86.5 2.2 fusion.23
  88.7 3.5 fusion.25
  93.3 3.4 collective-permute-start.7
  96.7 60.8 %all-gather.5.cloned.1.call-done = bf16[6144,128]{1,0:T(8,128)(2,1)} async-done(((bf16[384,128]{1,0:T(8,128)(2,1)}), bf16[6144,128]{1,0:T(8,128)(2,1)}) %all-gather.5.cloned.1.call-update) | async-done | bytes 1572880 | tf_op jit(solution)/shard_map/all_gather | solution.py:65
  157.5 2.2 fusion.21
  159.7 3.5 fusion.28
  164.4 3.5 collective-permute-start.10
  167.8 3.6 collective-permute-start.9
  171.4 3.6 collective-permute-start.12
  175.8 2.4 collective-permute-start.8
  179.0 2.2 collective-permute-start.11
  181.2 1.1 reshape.130
  182.3 2.6 collective-permute-done.8
  184.9 5.3 %collective-permute-done.11 = bf16[14,48,128]{2,0,1:T(8,128)(2,1)} collective-permute-done((bf16[14,48,128]{2,0,1:T(8,128)(2,1)}, bf16[14,48,128]{2,0,1:T(8,128)(2,1)}, u32[]{:S(2)}, u32[]{:S(2)}) %collective-permute-start.11) | collective-permute-done | bytes 172064 | tf_op jit(solution)/shard_map/ppermute | solution.py:11
  190.2 2.3 fusion.60
  192.5 1.9 collective-permute-start.14
  194.4 1.9 collective-permute-start.17
  196.3 5.1 %collective-permute-start.13 = (bf16[14,48,128]{2,0,1:T(8,128)(2,1)}, bf16[14,48,128]{2,0,1:T(8,128)(2,1)S(1)}, u32[]{:S(2)}, u32[]{:S(2)}) collective-permute-start(bf16[14,48,128]{2,0,1:T(8,128)(2,1)} %get-tuple-element.9), channel_id=1, source_target_pairs={{0,24},{8,0},{16,8},{24,16},{1,25},{9,1},{17,9},{25,17},{2,26},{10... | collective-permute-start | bytes 516104 | tf_op jit(solution)/shard_map/ppermute | solution.py:11
  201.5 3.9 %collective-permute-start.16 = (bf16[14,48,128]{2,0,1:T(8,128)(2,1)}, bf16[14,48,128]{2,0,1:T(8,128)(2,1)S(1)}, u32[]{:S(2)}, u32[]{:S(2)}) collective-permute-start(bf16[14,48,128]{2,0,1:T(8,128)(2,1)} %get-tuple-element.8), channel_id=1, source_target_pairs={{0,24},{8,0},{16,8},{24,16},{1,25},{9,1},{17,9},{25,17},{2,26},{10... | collective-permute-start | bytes 516104 | tf_op jit(solution)/shard_map/ppermute | solution.py:11
  205.4 1.9 collective-permute-start.15
  207.4 1.9 collective-permute-start.18
  209.3 4.8 %collective-permute-done.15 = bf16[14,48,128]{2,0,1:T(8,128)(2,1)S(1)} collective-permute-done((bf16[14,48,128]{2,0,1:T(8,128)(2,1)S(1)}, bf16[14,48,128]{2,0,1:T(8,128)(2,1)S(1)}, u32[]{:S(2)}, u32[]{:S(2)}) %collective-permute-start.15) | collective-permute-done | bytes 172064 | tf_op jit(solution)/shard_map/ppermute | solution.py:11
  214.2 2.1 collective-permute-done.18
  217.0 3.6 fusion.37
  221.4 2.5 fusion.16
  224.8 2.4 fusion.13
  227.2 1.4 copy-done.4
  228.6 2.9 fusion.11
  231.6 1.1 convolution_add_fusion
  232.7 3.4 fusion.31
  236.3 3.5 collective-permute-done.19
  239.9 1.7 collective-permute-start.23
  241.6 1.8 collective-permute-done.20
  243.4 3.5 collective-permute-done.21
  247.5 1.6 collective-permute-done.24
  249.1 3.1 collective-permute-start.25
  252.2 0.9 collective-permute-done.22
  253.1 0.9 collective-permute-done.25
  254.6 38.0 %reduce-scatter.5.cloned.1.call-done = bf16[384,128]{1,0:T(8,128)(2,1)} async-done(((bf16[6144,128]{1,0:T(8,128)(2,1)}), bf16[384,128]{1,0:T(8,128)(2,1)}) %reduce-scatter.5.cloned.1.call-update) | async-done | bytes 98320 | tf_op jit(solution)/shard_map/reduce_scatter | solution.py:116
  292.6 1.6 convert_multiply_fusion
  294.2 71.6 %reduce-scatter.3.cloned.1.call-done = bf16[384,128]{1,0:T(8,128)(2,1)} async-done(((bf16[6144,128]{1,0:T(8,128)(2,1)}), bf16[384,128]{1,0:T(8,128)(2,1)}) %reduce-scatter.3.cloned.1.call-update) | async-done | bytes 98320 | tf_op jit(solution)/shard_map/reduce_scatter | solution.py:116
  365.8 1.6 convert_multiply_fusion.1
  (93 shorter events, 13.2 us)
Async XLA Ops:
  7.2 79.3 %all-gather.3.cloned.1.call-start = ((), (), s32[]{:S(2)}) async-start(), calls=%async_computation.2 | async-start | bytes 1671168 | tf_op jit(solution)/shard_map/all_gather | solution.py:68
  7.9 149.6 %all-gather.5.cloned.1.call-start = ((), (), s32[]{:S(2)}) async-start(), calls=%async_computation.3 | async-start | bytes 1671168 | tf_op jit(solution)/shard_map/all_gather | solution.py:65
  7.9 3.1 collective-permute-start
  8.0 8.5 %collective-permute-start.3 = (bf16[24,1024]{1,0:T(8,128)(2,1)}, bf16[24,1024]{1,0:T(8,128)(2,1)S(1)}, u32[]{:S(2)}, u32[]{:S(2)}) collective-permute-start(bf16[24,1024]{1,0:T(8,128)(2,1)} %param.7), channel_id=1, source_target_pairs={{0,1},{1,2},{2,3},{3,4},{4,5},{5,6},{6,7},{7,0},{8,9},{9,10},{10,1... | collective-permute-start | bytes 147464 | tf_op jit(solution)/shard_map/ppermute | solution.py:11
  8.6 284.0 %reduce-scatter.5.cloned.1.call-start = ((), (), s32[]{:S(2)}) async-start(), calls=%async_computation.5 | async-start | bytes 1671168 | tf_op jit(solution)/shard_map/reduce_scatter | solution.py:116
  11.1 7.1 %collective-permute-start.1 = (bf16[24,1024]{1,0:T(8,128)(2,1)S(1)}, bf16[24,1024]{1,0:T(8,128)(2,1)S(1)}, u32[]{:S(2)}, u32[]{:S(2)}) collective-permute-start(bf16[24,1024]{1,0:T(8,128)(2,1)S(1)} %collective-permute-done), channel_id=1, source_target_pairs={{0,7},{1,0},{2,1},{3,2},{4,3},{5,4},{6,5},{7,6},{8,15},{9,8},{10,9... | collective-permute-start | bytes 147464 | tf_op jit(solution)/shard_map/ppermute | solution.py:11
  16.4 3.5 collective-permute-start.4
  18.2 5.3 %collective-permute-start.2 = (bf16[24,1024]{1,0:T(8,128)(2,1)S(1)}, bf16[24,1024]{1,0:T(8,128)(2,1)S(1)}, u32[]{:S(2)}, u32[]{:S(2)}) collective-permute-start(bf16[24,1024]{1,0:T(8,128)(2,1)S(1)} %collective-permute-done.1), channel_id=1, source_target_pairs={{0,7},{1,0},{2,1},{3,2},{4,3},{5,4},{6,5},{7,6},{8,15},{9,8},{10,9... | collective-permute-start | bytes 147464 | tf_op jit(solution)/shard_map/ppermute | solution.py:11
  20.0 3.5 collective-permute-start.5
  23.5 3.5 collective-permute-start.6
  93.3 81.8 %collective-permute-start.7 = (bf16[14,48,128]{2,0,1:T(8,128)(2,1)S(1)}, bf16[14,48,128]{2,0,1:T(8,128)(2,1)S(1)}, u32[]{:S(2)}, u32[]{:S(2)}) collective-permute-start(bf16[14,48,128]{2,0,1:T(8,128)(2,1)S(1)} %get-tuple-element.12), channel_id=1, source_target_pairs={{0,8},{8,16},{16,24},{24,0},{1,9},{9,17},{17,25},{25,1},{2,10},{10... | collective-permute-start | bytes 516104 | tf_op jit(solution)/shard_map/ppermute | solution.py:11
  163.6 14.6 %copy-start.5 = (bf16[14,4,48,128]{3,0,2,1:T(8,128)(2,1)}, bf16[14,4,48,128]{3,0,2,1:T(8,128)(2,1)S(1)}, u32[]{:S(2)}) copy-start(bf16[14,4,48,128]{3,0,2,1:T(8,128)(2,1)S(1)} %fusion.48) | copy-start | bytes 2064388
  164.4 13.8 %collective-permute-start.10 = (bf16[14,48,128]{2,0,1:T(8,128)(2,1)S(1)}, bf16[14,48,128]{2,0,1:T(8,128)(2,1)S(1)}, u32[]{:S(2)}, u32[]{:S(2)}) collective-permute-start(bf16[14,48,128]{2,0,1:T(8,128)(2,1)S(1)} %get-tuple-element.10), channel_id=1, source_target_pairs={{0,8},{8,16},{16,24},{24,0},{1,9},{9,17},{17,25},{25,1},{2,10},{10... | collective-permute-start | bytes 516104 | tf_op jit(solution)/shard_map/ppermute | solution.py:11
  167.8 14.4 %collective-permute-start.9 = (bf16[14,48,128]{2,0,1:T(8,128)(2,1)}, bf16[14,48,128]{2,0,1:T(8,128)(2,1)}, u32[]{:S(2)}, u32[]{:S(2)}) collective-permute-start(bf16[14,48,128]{2,0,1:T(8,128)(2,1)} %get-tuple-element.13), channel_id=1, source_target_pairs={{0,24},{8,0},{16,8},{24,16},{1,25},{9,1},{17,9},{25,17},{2,26},{10... | collective-permute-start | bytes 516104 | tf_op jit(solution)/shard_map/ppermute | solution.py:11
  171.4 10.9 %collective-permute-start.12 = (bf16[14,48,128]{2,0,1:T(8,128)(2,1)}, bf16[14,48,128]{2,0,1:T(8,128)(2,1)}, u32[]{:S(2)}, u32[]{:S(2)}) collective-permute-start(bf16[14,48,128]{2,0,1:T(8,128)(2,1)} %get-tuple-element.11), channel_id=1, source_target_pairs={{0,24},{8,0},{16,8},{24,16},{1,25},{9,1},{17,9},{25,17},{2,26},{10... | collective-permute-start | bytes 516104 | tf_op jit(solution)/shard_map/ppermute | solution.py:11
  175.8 9.1 %collective-permute-start.8 = (bf16[14,48,128]{2,0,1:T(8,128)(2,1)}, bf16[14,48,128]{2,0,1:T(8,128)(2,1)}, u32[]{:S(2)}, u32[]{:S(2)}) collective-permute-start(bf16[14,48,128]{2,0,1:T(8,128)(2,1)} %fusion.58), channel_id=1, source_target_pairs={{0,8},{8,16},{16,24},{24,0},{1,9},{9,17},{17,25},{25,1},{2,10},{10... | collective-permute-start | bytes 516104 | tf_op jit(solution)/shard_map/ppermute | solution.py:11
  179.0 11.2 %collective-permute-start.11 = (bf16[14,48,128]{2,0,1:T(8,128)(2,1)}, bf16[14,48,128]{2,0,1:T(8,128)(2,1)}, u32[]{:S(2)}, u32[]{:S(2)}) collective-permute-start(bf16[14,48,128]{2,0,1:T(8,128)(2,1)} %fusion.52), channel_id=1, source_target_pairs={{0,8},{8,16},{16,24},{24,0},{1,9},{9,17},{17,25},{25,1},{2,10},{10... | collective-permute-start | bytes 516104 | tf_op jit(solution)/shard_map/ppermute | solution.py:11
  192.5 12.9 %collective-permute-start.14 = (bf16[14,48,128]{2,0,1:T(8,128)(2,1)}, bf16[14,48,128]{2,0,1:T(8,128)(2,1)S(1)}, u32[]{:S(2)}, u32[]{:S(2)}) collective-permute-start(bf16[14,48,128]{2,0,1:T(8,128)(2,1)} %get-tuple-element.9), channel_id=1, source_target_pairs={{0,8},{8,16},{16,24},{24,0},{1,9},{9,17},{17,25},{25,1},{2,10},{10... | collective-permute-start | bytes 516104 | tf_op jit(solution)/shard_map/ppermute | solution.py:11
  194.4 12.9 %collective-permute-start.17 = (bf16[14,48,128]{2,0,1:T(8,128)(2,1)}, bf16[14,48,128]{2,0,1:T(8,128)(2,1)S(1)}, u32[]{:S(2)}, u32[]{:S(2)}) collective-permute-start(bf16[14,48,128]{2,0,1:T(8,128)(2,1)} %get-tuple-element.8), channel_id=1, source_target_pairs={{0,8},{8,16},{16,24},{24,0},{1,9},{9,17},{17,25},{25,1},{2,10},{10... | collective-permute-start | bytes 516104 | tf_op jit(solution)/shard_map/ppermute | solution.py:11
  196.3 13.0 %collective-permute-start.13 = (bf16[14,48,128]{2,0,1:T(8,128)(2,1)}, bf16[14,48,128]{2,0,1:T(8,128)(2,1)S(1)}, u32[]{:S(2)}, u32[]{:S(2)}) collective-permute-start(bf16[14,48,128]{2,0,1:T(8,128)(2,1)} %get-tuple-element.9), channel_id=1, source_target_pairs={{0,24},{8,0},{16,8},{24,16},{1,25},{9,1},{17,9},{25,17},{2,26},{10... | collective-permute-start | bytes 516104 | tf_op jit(solution)/shard_map/ppermute | solution.py:11
  201.5 7.8 %collective-permute-start.16 = (bf16[14,48,128]{2,0,1:T(8,128)(2,1)}, bf16[14,48,128]{2,0,1:T(8,128)(2,1)S(1)}, u32[]{:S(2)}, u32[]{:S(2)}) collective-permute-start(bf16[14,48,128]{2,0,1:T(8,128)(2,1)} %get-tuple-element.8), channel_id=1, source_target_pairs={{0,24},{8,0},{16,8},{24,16},{1,25},{9,1},{17,9},{25,17},{2,26},{10... | collective-permute-start | bytes 516104 | tf_op jit(solution)/shard_map/ppermute | solution.py:11
  205.4 8.8 %collective-permute-start.15 = (bf16[14,48,128]{2,0,1:T(8,128)(2,1)S(1)}, bf16[14,48,128]{2,0,1:T(8,128)(2,1)S(1)}, u32[]{:S(2)}, u32[]{:S(2)}) collective-permute-start(bf16[14,48,128]{2,0,1:T(8,128)(2,1)S(1)} %collective-permute-done.14), channel_id=1, source_target_pairs={{0,8},{8,16},{16,24},{24,0},{1,9},{9,17},{17,25},{25,1},{2,10},{10... | collective-permute-start | bytes 516104 | tf_op jit(solution)/shard_map/ppermute | solution.py:11
  207.4 8.9 %collective-permute-start.18 = (bf16[14,48,128]{2,0,1:T(8,128)(2,1)S(1)}, bf16[14,48,128]{2,0,1:T(8,128)(2,1)S(1)}, u32[]{:S(2)}, u32[]{:S(2)}) collective-permute-start(bf16[14,48,128]{2,0,1:T(8,128)(2,1)S(1)} %collective-permute-done.17), channel_id=1, source_target_pairs={{0,8},{8,16},{16,24},{24,0},{1,9},{9,17},{17,25},{25,1},{2,10},{10... | collective-permute-start | bytes 516104 | tf_op jit(solution)/shard_map/ppermute | solution.py:11
  209.3 7.0 %copy-start.6 = (bf16[14,48,128]{2,0,1:T(8,128)(2,1)}, bf16[14,48,128]{2,0,1:T(8,128)(2,1)S(1)}, u32[]{:S(2)}) copy-start(bf16[14,48,128]{2,0,1:T(8,128)(2,1)S(1)} %collective-permute-done.13) | copy-start | bytes 516100
  209.3 7.0 %copy-start.7 = (bf16[14,48,128]{2,0,1:T(8,128)(2,1)}, bf16[14,48,128]{2,0,1:T(8,128)(2,1)S(1)}, u32[]{:S(2)}) copy-start(bf16[14,48,128]{2,0,1:T(8,128)(2,1)S(1)} %collective-permute-done.16) | copy-start | bytes 516100
  214.2 2.1 copy-start.8
  216.3 0.7 copy-start.9
  221.4 2.5 copy-start
  223.9 141.8 %reduce-scatter.3.cloned.1.call-start = ((), (), s32[]{:S(2)}) async-start(), calls=%async_computation.4 | async-start | bytes 1671168 | tf_op jit(solution)/shard_map/reduce_scatter | solution.py:116
  224.8 2.4 copy-start.2
  227.2 1.4 copy-start.4
  228.6 2.9 copy-start.1
  228.6 3.0 copy-start.3
  236.3 3.5 collective-permute-start.19
  239.9 3.5 collective-permute-start.20
  239.9 3.5 collective-permute-start.23
  243.4 3.5 collective-permute-start.21
  247.0 2.1 collective-permute-start.24
  247.3 5.8 %collective-permute-start.22 = (bf16[8,24,128]{2,0,1:T(8,128)(2,1)S(1)}, bf16[8,24,128]{2,0,1:T(8,128)(2,1)S(1)}, u32[]{:S(2)}, u32[]{:S(2)}) collective-permute-start(bf16[8,24,128]{2,0,1:T(8,128)(2,1)S(1)} %get-tuple-element.14), channel_id=1, source_target_pairs={{0,1},{1,2},{2,3},{3,4},{4,5},{5,6},{6,7},{7,0},{8,9},{9,10},{10,1... | collective-permute-start | bytes 147464 | tf_op jit(solution)/shard_map/ppermute | solution.py:11
  249.1 4.9 %collective-permute-start.25 = (bf16[8,24,128]{2,0,1:T(8,128)(2,1)S(1)}, bf16[8,24,128]{2,0,1:T(8,128)(2,1)S(1)}, u32[]{:S(2)}, u32[]{:S(2)}) collective-permute-start(bf16[8,24,128]{2,0,1:T(8,128)(2,1)S(1)} %fusion.61), channel_id=1, source_target_pairs={{0,7},{1,0},{2,1},{3,2},{4,3},{5,4},{6,5},{7,6},{8,15},{9,8},{10,9... | collective-permute-start | bytes 147464 | tf_op jit(solution)/shard_map/ppermute | solution.py:11
Sparse Core Ops, SparseCore 0:
  10.0 76.3 all-gather.2
  88.6 68.9 all-gather.4
  224.1 68.5 reduce-scatter.4
  295.3 70.4 reduce-scatter.2
where the time goes:
time: 375 us; the launch traced here: 374 us
  waiting for transfers between devices  265 us (71%)
  starting transfers between devices  48.7 us (13%)
  matrix products  26.1 us (7%)
  between operations  14.3 us (4%)
  other arithmetic  12.8 us (3%)
  local copies, waits for them, and re-layouts  7.4 us (2%)
    reduce_scatter x2, waiting for transfers between devices, slot_grad(): lax.psum_scatter(slot_dw.reshape(cap * bs, bs), 'dp', scatter_dimension=0...  110 us
    all_gather x1, waiting for transfers between devices, on_device(): lax.all_gather(gate_slots[0, 0].reshape(per_dev * bs, bs), 'dp', axis=0,...  60.8 us
    all_gather x1, waiting for transfers between devices, on_device(): lax.all_gather(up_slots[0, 0].reshape(per_dev * bs, bs), 'dp', axis=0, ti...  57.6 us
    ppermute x26, starting transfers between devices, _shift(): return lax.ppermute(x, axis, perm=[(i, (i + step) % n) for i in range(n)])  48.5 us
    ppermute x26, waiting for transfers between devices, _shift(): return lax.ppermute(x, axis, perm=[(i, (i + step) % n) for i in range(n)])  35.6 us
  transfers between devices with their start and end apart: 30, of which 17 were waited for; matrix products, arithmetic and copies ran while one was open for 9% of the time, Pallas kernels for 0%

commit v1 on v0

--- a/solution.py
+++ b/solution.py
@@ -2,6 +2,7 @@
 import jax.numpy as jnp
 from jax import lax
 from jax.sharding import PartitionSpec as P
+from jax.lax import axis_index, axis_size, ppermute
 
 F32 = jnp.float32
 BF16 = jnp.bfloat16
@@ -62,9 +63,36 @@
     tok = layer_input.shape[0] * n_col
     rows_per = tok // n_row
     cols_per = tok // n_col
-    gate_all = lax.all_gather(
-        gate_slots[0, 0].reshape(per_dev * bs, bs), "dp", axis=0, tiled=True
-    ).reshape(cap, bs, bs)
+
+    def trace_paths(shard_in):
+        piece_out = axis_index("dp")
+        s_next = axis_size("dp")
+        latest, piece_next, clean = (s_next, piece_out, shard_in.shape[0])
+        inbox = [(hop_no, (hop_no + 1) % latest) for hop_no in range(latest)]
+        so_far_all = [(hop_no, (hop_no - 1) % latest) for hop_no in range(latest)]
+        current_value = jnp.zeros(
+            (*shard_in.shape[:0], latest * clean, *shard_in.shape[1:]), shard_in.dtype
+        )
+        prior = formed = shard_in
+        known = latest // 2
+        current_value = lax.dynamic_update_slice_in_dim(
+            current_value, shard_in, piece_next * clean, axis=0
+        )
+        at = 1
+        while at < known + 1:
+            prior = ppermute(prior, axis_name="dp", perm=inbox)
+            current_value = lax.dynamic_update_slice_in_dim(
+                current_value, prior, (piece_next - at) % latest * clean, axis=0
+            )
+            if at < latest - known:
+                formed = ppermute(formed, axis_name="dp", perm=so_far_all)
+                current_value = lax.dynamic_update_slice_in_dim(
+                    current_value, formed, (piece_next + at) % latest * clean, axis=0
+                )
+            at += 1
+        return current_value
+
+    gate_all = trace_paths(gate_slots[0, 0].reshape(per_dev * bs, bs)).reshape(cap, bs, bs)
     up_all = lax.all_gather(
         up_slots[0, 0].reshape(per_dev * bs, bs), "dp", axis=0, tiled=True
     ).reshape(cap, bs, bs)

time: 375 us -> 323 us (0.86)
  the two profiles are of different devices: /device:TPU:2 before, /device:TPU:14 now
where the time goes in v1:
time: 323 us; the launch traced here: 322 us
  waiting for transfers between devices  145 us (45%)
  starting transfers between devices  115 us (36%)
  matrix products  24.7 us (8%)
  between operations  15 us (5%)
  other arithmetic  12.7 us (4%)
  local copies, waits for them, and re-layouts  10.3 us (3%)
    reduce_scatter x2, waiting for transfers between devices, slot_grad(): lax.psum_scatter(slot_dw.reshape(cap * bs, bs), 'dp', scatter_dimension=0...  112 us
    ppermute x26, starting transfers between devices, _shift(): return lax.ppermute(x, axis, perm=[(i, (i + step) % n) for i in range(n)])  55.7 us
    ppermute x7, starting transfers between devices, trace_paths(): formed = ppermute(formed, axis_name='dp', perm=so_far_all)  41.4 us
    ppermute x26, waiting for transfers between devices, _shift(): return lax.ppermute(x, axis, perm=[(i, (i + step) % n) for i in range(n)])  24 us
    ppermute x8, starting transfers between devices, trace_paths(): prior = ppermute(prior, axis_name='dp', perm=inbox)  17.2 us
    ppermute x8, waiting for transfers between devices, trace_paths(): prior = ppermute(prior, axis_name='dp', perm=inbox)  8.3 us
    dot_general x2, matrix products, pre_rows(): jnp.einsum('qc,qtn->ctn', col_pick.astype(F32), per_slot, precision=high,...  7.03 us
    unnamed x45, local copies, waits for them, and re-layouts  6.84 us
  transfers between devices with their start and end apart: 44, of which 19 were waited for; matrix products, arithmetic and copies ran while one was open for 10% of the time, Pallas kernels for 0%

profile of v1, /device:TPU:14, one launch (start us, length us, event | category | flops | bytes accessed | tf_op | source)
XLA Modules:
  0.0 322.0 jit_solution(14177289933173362368)
XLA Ops:
  7.2 3.8 %collective-permute-start.10 = (bf16[384,128]{1,0:T(8,128)(2,1)}, bf16[384,128]{1,0:T(8,128)(2,1)S(1)}, u32[]{:S(2)}, u32[]{:S(2)}) collective-permute-start(bf16[384,128]{1,0:T(8,128)(2,1)} %bitcast.166), channel_id=1, source_target_pairs={{0,32},{32,64},{64,96},{96,128},{128,160},{160,192},{192,224},{224... | collective-permute-start | bytes 294920 | tf_op jit(solution)/shard_map/ppermute | solution.py:83
  11.1 9.5 %collective-permute-start.11 = (bf16[384,128]{1,0:T(8,128)(2,1)}, bf16[384,128]{1,0:T(8,128)(2,1)S(1)}, u32[]{:S(2)}, u32[]{:S(2)}) collective-permute-start(bf16[384,128]{1,0:T(8,128)(2,1)} %bitcast.167), channel_id=1, source_target_pairs={{0,480},{32,0},{64,32},{96,64},{128,96},{160,128},{192,160},{224,1... | collective-permute-start | bytes 294920 | tf_op jit(solution)/shard_map/ppermute | solution.py:88
  26.2 1.9 collective-permute-start.12
  28.1 5.1 %collective-permute-start.13 = (bf16[384,128]{1,0:T(8,128)(2,1)S(1)}, bf16[384,128]{1,0:T(8,128)(2,1)S(1)}, u32[]{:S(2)}, u32[]{:S(2)}) collective-permute-start(bf16[384,128]{1,0:T(8,128)(2,1)S(1)} %collective-permute-done.11), channel_id=1, source_target_pairs={{0,480},{32,0},{64,32},{96,64},{128,96},{160,128},{192,160},{224,1... | collective-permute-start | bytes 294920 | tf_op jit(solution)/shard_map/ppermute | solution.py:88
  33.7 2.0 collective-permute-start.5
  37.2 2.6 collective-permute-start.6
  41.0 1.9 collective-permute-start.14
  42.9 5.1 %collective-permute-start.15 = (bf16[384,128]{1,0:T(8,128)(2,1)S(1)}, bf16[384,128]{1,0:T(8,128)(2,1)S(1)}, u32[]{:S(2)}, u32[]{:S(2)}) collective-permute-start(bf16[384,128]{1,0:T(8,128)(2,1)S(1)} %collective-permute-done.13), channel_id=1, source_target_pairs={{0,480},{32,0},{64,32},{96,64},{128,96},{160,128},{192,160},{224,1... | collective-permute-start | bytes 294920 | tf_op jit(solution)/shard_map/ppermute | solution.py:88
  50.7 1.9 collective-permute-start.16
  52.7 5.1 %collective-permute-start.17 = (bf16[384,128]{1,0:T(8,128)(2,1)S(1)}, bf16[384,128]{1,0:T(8,128)(2,1)S(1)}, u32[]{:S(2)}, u32[]{:S(2)}) collective-permute-start(bf16[384,128]{1,0:T(8,128)(2,1)S(1)} %collective-permute-done.15), channel_id=1, source_target_pairs={{0,480},{32,0},{64,32},{96,64},{128,96},{160,128},{192,160},{224,1... | collective-permute-start | bytes 294920 | tf_op jit(solution)/shard_map/ppermute | solution.py:88
  58.4 1.9 collective-permute-start.18
  60.4 5.5 %collective-permute-start.19 = (bf16[384,128]{1,0:T(8,128)(2,1)S(1)}, bf16[384,128]{1,0:T(8,128)(2,1)S(1)}, u32[]{:S(2)}, u32[]{:S(2)}) collective-permute-start(bf16[384,128]{1,0:T(8,128)(2,1)S(1)} %collective-permute-done.17), channel_id=1, source_target_pairs={{0,480},{32,0},{64,32},{96,64},{128,96},{160,128},{192,160},{224,1... | collective-permute-start | bytes 294920 | tf_op jit(solution)/shard_map/ppermute | solution.py:88
  66.4 1.9 collective-permute-start.20
  68.3 5.4 %collective-permute-start.21 = (bf16[384,128]{1,0:T(8,128)(2,1)S(1)}, bf16[384,128]{1,0:T(8,128)(2,1)S(1)}, u32[]{:S(2)}, u32[]{:S(2)}) collective-permute-start(bf16[384,128]{1,0:T(8,128)(2,1)S(1)} %collective-permute-done.19), channel_id=1, source_target_pairs={{0,480},{32,0},{64,32},{96,64},{128,96},{160,128},{192,160},{224,1... | collective-permute-start | bytes 294920 | tf_op jit(solution)/shard_map/ppermute | solution.py:88
  76.2 5.6 %collective-permute-start.23 = (bf16[384,128]{1,0:T(8,128)(2,1)S(1)}, bf16[384,128]{1,0:T(8,128)(2,1)S(1)}, u32[]{:S(2)}, u32[]{:S(2)}) collective-permute-start(bf16[384,128]{1,0:T(8,128)(2,1)S(1)} %collective-permute-done.21), channel_id=1, source_target_pairs={{0,480},{32,0},{64,32},{96,64},{128,96},{160,128},{192,160},{224,1... | collective-permute-start | bytes 294920 | tf_op jit(solution)/shard_map/ppermute | solution.py:88
  82.4 1.9 collective-permute-start.24
  84.3 6.3 %collective-permute-done.24 = bf16[384,128]{1,0:T(8,128)(2,1)S(1)} collective-permute-done((bf16[384,128]{1,0:T(8,128)(2,1)S(1)}, bf16[384,128]{1,0:T(8,128)(2,1)S(1)}, u32[]{:S(2)}, u32[]{:S(2)}) %collective-permute-start.24) | collective-permute-done | bytes 98336 | tf_op jit(solution)/shard_map/ppermute | solution.py:83
  91.4 3.5 %fusion.28 = bf16[14,192,128]{2,0,1:T(8,128)(2,1)S(1)} fusion(f32[48,192,128]{2,1,0:T(8,128)S(1)} %fusion.21, bf16[48,14]{0,1:T(8,128)(2,1)S(1)} %get-tuple-element.4), kind=kOutput, calls=%fused_computation.46 | convolution fusion | flops 99434496 | bytes 5408064 | tf_op jit(solution)/shard_map/qc,qtn->ctn/dot_general | solution.py:116
  96.0 3.7 %collective-permute-start.25 = (bf16[14,48,128]{2,0,1:T(8,128)(2,1)S(1)}, bf16[14,48,128]{2,0,1:T(8,128)(2,1)S(1)}, u32[]{:S(2)}, u32[]{:S(2)}) collective-permute-start(bf16[14,48,128]{2,0,1:T(8,128)(2,1)S(1)} %get-tuple-element.12), channel_id=1, source_target_pairs={{0,8},{8,16},{16,24},{24,0},{1,9},{9,17},{17,25},{25,1},{2,10},{10... | collective-permute-start | bytes 516104 | tf_op jit(solution)/shard_map/ppermute | solution.py:12
  99.7 2.3 collective-permute-start.27
  102.1 2.2 fusion.23
  104.3 3.5 %fusion.25 = bf16[14,192,128]{2,0,1:T(8,128)(2,1)S(1)} fusion(f32[48,192,128]{2,1,0:T(8,128)S(1)} %fusion.23, bf16[48,14]{0,1:T(8,128)(2,1)S(1)} %get-tuple-element.4), kind=kOutput, calls=%fused_computation.45 | convolution fusion | flops 99434496 | bytes 5408064 | tf_op jit(solution)/shard_map/qc,qtn->ctn/dot_general | solution.py:116
  108.9 3.7 %collective-permute-start.7 = (bf16[14,48,128]{2,0,1:T(8,128)(2,1)S(1)}, bf16[14,48,128]{2,0,1:T(8,128)(2,1)S(1)}, u32[]{:S(2)}, u32[]{:S(2)}) collective-permute-start(bf16[14,48,128]{2,0,1:T(8,128)(2,1)S(1)} %get-tuple-element.10), channel_id=1, source_target_pairs={{0,8},{8,16},{16,24},{24,0},{1,9},{9,17},{17,25},{25,1},{2,10},{10... | collective-permute-start | bytes 516104 | tf_op jit(solution)/shard_map/ppermute | solution.py:12
  113.4 3.3 %collective-permute-start.26 = (bf16[14,48,128]{2,0,1:T(8,128)(2,1)}, bf16[14,48,128]{2,0,1:T(8,128)(2,1)}, u32[]{:S(2)}, u32[]{:S(2)}) collective-permute-start(bf16[14,48,128]{2,0,1:T(8,128)(2,1)} %fusion.52), channel_id=1, source_target_pairs={{0,8},{8,16},{16,24},{24,0},{1,9},{9,17},{17,25},{25,1},{2,10},{10... | collective-permute-start | bytes 516104 | tf_op jit(solution)/shard_map/ppermute | solution.py:12
  116.8 2.5 collective-permute-start.9
  120.0 3.3 %collective-permute-start.8 = (bf16[14,48,128]{2,0,1:T(8,128)(2,1)}, bf16[14,48,128]{2,0,1:T(8,128)(2,1)}, u32[]{:S(2)}, u32[]{:S(2)}) collective-permute-start(bf16[14,48,128]{2,0,1:T(8,128)(2,1)} %fusion.58), channel_id=1, source_target_pairs={{0,8},{8,16},{16,24},{24,0},{1,9},{9,17},{17,25},{25,1},{2,10},{10... | collective-permute-start | bytes 516104 | tf_op jit(solution)/shard_map/ppermute | solution.py:12
  125.4 3.8 %collective-permute-done.8 = bf16[14,48,128]{2,0,1:T(8,128)(2,1)} collective-permute-done((bf16[14,48,128]{2,0,1:T(8,128)(2,1)}, bf16[14,48,128]{2,0,1:T(8,128)(2,1)}, u32[]{:S(2)}, u32[]{:S(2)}) %collective-permute-start.8) | collective-permute-done | bytes 172064 | tf_op jit(solution)/shard_map/ppermute | solution.py:12
  129.2 2.3 fusion.57
  131.5 2.5 collective-permute-start.29
  134.0 3.6 %collective-permute-start.32 = (bf16[14,48,128]{2,0,1:T(8,128)(2,1)}, bf16[14,48,128]{2,0,1:T(8,128)(2,1)S(1)}, u32[]{:S(2)}, u32[]{:S(2)}) collective-permute-start(bf16[14,48,128]{2,0,1:T(8,128)(2,1)} %get-tuple-element.9), channel_id=1, source_target_pairs={{0,8},{8,16},{16,24},{24,0},{1,9},{9,17},{17,25},{25,1},{2,10},{10... | collective-permute-start | bytes 516104 | tf_op jit(solution)/shard_map/ppermute | solution.py:12
  137.7 2.5 collective-permute-start.28
  140.2 5.1 %collective-permute-start.31 = (bf16[14,48,128]{2,0,1:T(8,128)(2,1)}, bf16[14,48,128]{2,0,1:T(8,128)(2,1)S(1)}, u32[]{:S(2)}, u32[]{:S(2)}) collective-permute-start(bf16[14,48,128]{2,0,1:T(8,128)(2,1)} %get-tuple-element.9), channel_id=1, source_target_pairs={{0,24},{8,0},{16,8},{24,16},{1,25},{9,1},{17,9},{25,17},{2,26},{10... | collective-permute-start | bytes 516104 | tf_op jit(solution)/shard_map/ppermute | solution.py:12
  145.4 1.9 collective-permute-start.30
  147.3 3.3 %collective-permute-start.33 = (bf16[14,48,128]{2,0,1:T(8,128)(2,1)S(1)}, bf16[14,48,128]{2,0,1:T(8,128)(2,1)S(1)}, u32[]{:S(2)}, u32[]{:S(2)}) collective-permute-start(bf16[14,48,128]{2,0,1:T(8,128)(2,1)S(1)} %collective-permute-done.32), channel_id=1, source_target_pairs={{0,8},{8,16},{16,24},{24,0},{1,9},{9,17},{17,25},{25,1},{2,10},{10... | collective-permute-start | bytes 516104 | tf_op jit(solution)/shard_map/ppermute | solution.py:12
  150.7 3.3 %collective-permute-done.30 = bf16[14,48,128]{2,0,1:T(8,128)(2,1)S(1)} collective-permute-done((bf16[14,48,128]{2,0,1:T(8,128)(2,1)S(1)}, bf16[14,48,128]{2,0,1:T(8,128)(2,1)S(1)}, u32[]{:S(2)}, u32[]{:S(2)}) %collective-permute-start.30) | collective-permute-done | bytes 172064 | tf_op jit(solution)/shard_map/ppermute | solution.py:12
  154.0 2.1 collective-permute-done.33
  156.8 3.5 %fusion.37 = (bf16[14,4,48,128]{3,0,2,1:T(8,128)(2,1)S(1)}, bf16[14,4,48,128]{3,0,2,1:T(8,128)(2,1)S(1)}) fusion(s32[]{:T(128)S(6)} %select_n.194, bf16[14,1,48,128]{3,0,2,1:T(8,128)(2,1)} %bitcast.30, bf16[14,1,48,128]{3,0,2,1:T(8,128)(2,1)} %bitcast.163, bf16[14,1,48,128]{3,0,2,1:T(8,128)(2,1)} %bitcast.165, bf16[14,1,48,128]{3,0,2,1:T(8,128)(2,1)S(1)} %bitcast.162, ...), kind=kLoop, calls=%fused_computation.51 | loop fusion | flops 4816896 | bytes 2752516 | tf_op jit(solution)/shard_map/jit(_roll_dynamic)/concatenate | solution.py:135
  162.5 2.4 fusion.16
  166.1 2.4 fusion.13
  169.9 2.9 fusion.8
  174.0 3.4 %fusion.31 = bf16[8,192,128]{2,0,1:T(8,128)(2,1)S(1)} fusion(f32[48,192,128]{2,1,0:T(8,128)S(1)} %convolution_add_fusion, bf16[48,8]{0,1:T(8,128)(2,1)S(1)} %get-tuple-element.5), kind=kOutput, calls=%fused_computation.47 | convolution fusion | flops 56819712 | bytes 5112576 | tf_op jit(solution)/shard_map/qr,qtk->rtk/dot_general | solution.py:155
  177.6 3.5 %collective-permute-done.34 = bf16[8,24,128]{2,0,1:T(8,128)(2,1)S(1)} collective-permute-done((bf16[8,24,128]{2,0,1:T(8,128)(2,1)S(1)}, bf16[8,24,128]{2,0,1:T(8,128)(2,1)S(1)}, u32[]{:S(2)}, u32[]{:S(2)}) %collective-permute-start.34) | collective-permute-done | bytes 49184 | tf_op jit(solution)/shard_map/ppermute | solution.py:12
  181.2 2.6 collective-permute-start.35
  184.7 3.8 %collective-permute-start.36 = (bf16[8,24,128]{2,0,1:T(8,128)(2,1)S(1)}, bf16[8,24,128]{2,0,1:T(8,128)(2,1)S(1)}, u32[]{:S(2)}, u32[]{:S(2)}) collective-permute-start(bf16[8,24,128]{2,0,1:T(8,128)(2,1)S(1)} %fusion.66), channel_id=1, source_target_pairs={{0,1},{1,2},{2,3},{3,4},{4,5},{5,6},{6,7},{7,0},{8,9},{9,10},{10,1... | collective-permute-start | bytes 147464 | tf_op jit(solution)/shard_map/ppermute | solution.py:12
  189.4 3.9 %collective-permute-start.37 = (bf16[8,24,128]{2,0,1:T(8,128)(2,1)S(1)}, bf16[8,24,128]{2,0,1:T(8,128)(2,1)S(1)}, u32[]{:S(2)}, u32[]{:S(2)}) collective-permute-start(bf16[8,24,128]{2,0,1:T(8,128)(2,1)S(1)} %get-tuple-element.14), channel_id=1, source_target_pairs={{0,1},{1,2},{2,3},{3,4},{4,5},{5,6},{6,7},{7,0},{8,9},{9,10},{10,1... | collective-permute-start | bytes 147464 | tf_op jit(solution)/shard_map/ppermute | solution.py:12
  194.1 5.2 %collective-permute-done.40 = bf16[8,24,128]{2,0,1:T(8,128)(2,1)S(1)} collective-permute-done((bf16[8,24,128]{2,0,1:T(8,128)(2,1)S(1)}, bf16[8,24,128]{2,0,1:T(8,128)(2,1)S(1)}, u32[]{:S(2)}, u32[]{:S(2)}) %collective-permute-start.40) | collective-permute-done | bytes 49184 | tf_op jit(solution)/shard_map/ppermute | solution.py:12
  200.0 40.6 %reduce-scatter.5.cloned.1.call-done = bf16[384,128]{1,0:T(8,128)(2,1)} async-done(((bf16[6144,128]{1,0:T(8,128)(2,1)}), bf16[384,128]{1,0:T(8,128)(2,1)}) %reduce-scatter.5.cloned.1.call-update) | async-done | bytes 98320 | tf_op jit(solution)/shard_map/reduce_scatter | solution.py:144
  242.1 71.7 %reduce-scatter.3.cloned.1.call-done = bf16[384,128]{1,0:T(8,128)(2,1)} async-done(((bf16[6144,128]{1,0:T(8,128)(2,1)}), bf16[384,128]{1,0:T(8,128)(2,1)}) %reduce-scatter.3.cloned.1.call-update) | async-done | bytes 98320 | tf_op jit(solution)/shard_map/reduce_scatter | solution.py:144
  (145 shorter events, 34.9 us)
Async XLA Ops:
  7.2 16.6 %copy-start.13 = (bf16[1,1,3,128,128]{4,3,2,1,0:T(8,128)(2,1)S(1)}, bf16[1,1,3,128,128]{4,3,2,1,0:T(8,128)(2,1)}, u32[]{:S(2)}) copy-start(bf16[1,1,3,128,128]{4,3,2,1,0:T(8,128)(2,1)} %param.9) | copy-start | bytes 294916
  7.2 94.9 %all-gather.2.cloned.1.call-start = ((), (), s32[]{:S(2)}) async-start(), calls=%async_computation.2 | async-start | bytes 1671168 | tf_op jit(solution)/shard_map/all_gather | solution.py:96
  7.2 19.0 %collective-permute-start.10 = (bf16[384,128]{1,0:T(8,128)(2,1)}, bf16[384,128]{1,0:T(8,128)(2,1)S(1)}, u32[]{:S(2)}, u32[]{:S(2)}) collective-permute-start(bf16[384,128]{1,0:T(8,128)(2,1)} %bitcast.166), channel_id=1, source_target_pairs={{0,32},{32,64},{64,96},{96,128},{128,160},{160,192},{192,224},{224... | collective-permute-start | bytes 294920 | tf_op jit(solution)/shard_map/ppermute | solution.py:83
  11.1 17.0 %collective-permute-start.11 = (bf16[384,128]{1,0:T(8,128)(2,1)}, bf16[384,128]{1,0:T(8,128)(2,1)S(1)}, u32[]{:S(2)}, u32[]{:S(2)}) collective-permute-start(bf16[384,128]{1,0:T(8,128)(2,1)} %bitcast.167), channel_id=1, source_target_pairs={{0,480},{32,0},{64,32},{96,64},{128,96},{160,128},{192,160},{224,1... | collective-permute-start | bytes 294920 | tf_op jit(solution)/shard_map/ppermute | solution.py:88
  20.6 3.5 %collective-permute-start = (bf16[24,1024]{1,0:T(8,128)(2,1)}, bf16[24,1024]{1,0:T(8,128)(2,1)S(1)}, u32[]{:S(2)}, u32[]{:S(2)}) collective-permute-start(bf16[24,1024]{1,0:T(8,128)(2,1)} %param.7), channel_id=1, source_target_pairs={{0,7},{1,0},{2,1},{3,2},{4,3},{5,4},{6,5},{7,6},{8,15},{9,8},{10,9... | collective-permute-start | bytes 147464 | tf_op jit(solution)/shard_map/ppermute | solution.py:12
  20.6 4.8 %collective-permute-start.3 = (bf16[24,1024]{1,0:T(8,128)(2,1)}, bf16[24,1024]{1,0:T(8,128)(2,1)S(1)}, u32[]{:S(2)}, u32[]{:S(2)}) collective-permute-start(bf16[24,1024]{1,0:T(8,128)(2,1)} %param.7), channel_id=1, source_target_pairs={{0,1},{1,2},{2,3},{3,4},{4,5},{5,6},{6,7},{7,0},{8,9},{9,10},{10,1... | collective-permute-start | bytes 147464 | tf_op jit(solution)/shard_map/ppermute | solution.py:12
  21.1 219.4 %reduce-scatter.5.cloned.1.call-start = ((), (), s32[]{:S(2)}) async-start(), calls=%async_computation.4 | async-start | bytes 1671168 | tf_op jit(solution)/shard_map/reduce_scatter | solution.py:144
  23.5 17.3 %copy-start.9 = (bf16[24,1024]{1,0:T(8,128)(2,1)S(1)}, bf16[24,1024]{1,0:T(8,128)(2,1)}, u32[]{:S(2)}) copy-start(bf16[24,1024]{1,0:T(8,128)(2,1)} %param.7) | copy-start | bytes 147460
  24.1 9.1 %collective-permute-start.1 = (bf16[24,1024]{1,0:T(8,128)(2,1)S(1)}, bf16[24,1024]{1,0:T(8,128)(2,1)S(1)}, u32[]{:S(2)}, u32[]{:S(2)}) collective-permute-start(bf16[24,1024]{1,0:T(8,128)(2,1)S(1)} %collective-permute-done), channel_id=1, source_target_pairs={{0,7},{1,0},{2,1},{3,2},{4,3},{5,4},{6,5},{7,6},{8,15},{9,8},{10,9... | collective-permute-start | bytes 147464 | tf_op jit(solution)/shard_map/ppermute | solution.py:12
  25.4 8.3 %collective-permute-start.4 = (bf16[24,1024]{1,0:T(8,128)(2,1)S(1)}, bf16[24,1024]{1,0:T(8,128)(2,1)S(1)}, u32[]{:S(2)}, u32[]{:S(2)}) collective-permute-start(bf16[24,1024]{1,0:T(8,128)(2,1)S(1)} %collective-permute-done.3), channel_id=1, source_target_pairs={{0,1},{1,2},{2,3},{3,4},{4,5},{5,6},{6,7},{7,0},{8,9},{9,10},{10,1... | collective-permute-start | bytes 147464 | tf_op jit(solution)/shard_map/ppermute | solution.py:12
  26.2 14.8 %collective-permute-start.12 = (bf16[384,128]{1,0:T(8,128)(2,1)S(1)}, bf16[384,128]{1,0:T(8,128)(2,1)S(1)}, u32[]{:S(2)}, u32[]{:S(2)}) collective-permute-start(bf16[384,128]{1,0:T(8,128)(2,1)S(1)} %collective-permute-done.10), channel_id=1, source_target_pairs={{0,32},{32,64},{64,96},{96,128},{128,160},{160,192},{192,224},{224... | collective-permute-start | bytes 294920 | tf_op jit(solution)/shard_map/ppermute | solution.py:83
  28.1 14.8 %collective-permute-start.13 = (bf16[384,128]{1,0:T(8,128)(2,1)S(1)}, bf16[384,128]{1,0:T(8,128)(2,1)S(1)}, u32[]{:S(2)}, u32[]{:S(2)}) collective-permute-start(bf16[384,128]{1,0:T(8,128)(2,1)S(1)} %collective-permute-done.11), channel_id=1, source_target_pairs={{0,480},{32,0},{64,32},{96,64},{128,96},{160,128},{192,160},{224,1... | collective-permute-start | bytes 294920 | tf_op jit(solution)/shard_map/ppermute | solution.py:88
  33.3 6.5 %collective-permute-start.2 = (bf16[24,1024]{1,0:T(8,128)(2,1)S(1)}, bf16[24,1024]{1,0:T(8,128)(2,1)S(1)}, u32[]{:S(2)}, u32[]{:S(2)}) collective-permute-start(bf16[24,1024]{1,0:T(8,128)(2,1)S(1)} %collective-permute-done.1), channel_id=1, source_target_pairs={{0,7},{1,0},{2,1},{3,2},{4,3},{5,4},{6,5},{7,6},{8,15},{9,8},{10,9... | collective-permute-start | bytes 147464 | tf_op jit(solution)/shard_map/ppermute | solution.py:12
  33.7 3.5 %collective-permute-start.5 = (bf16[24,1024]{1,0:T(8,128)(2,1)S(1)}, bf16[24,1024]{1,0:T(8,128)(2,1)S(1)}, u32[]{:S(2)}, u32[]{:S(2)}) collective-permute-start(bf16[24,1024]{1,0:T(8,128)(2,1)S(1)} %collective-permute-done.4), channel_id=1, source_target_pairs={{0,1},{1,2},{2,3},{3,4},{4,5},{5,6},{6,7},{7,0},{8,9},{9,10},{10,1... | collective-permute-start | bytes 147464 | tf_op jit(solution)/shard_map/ppermute | solution.py:12
  37.2 3.5 %collective-permute-start.6 = (bf16[24,1024]{1,0:T(8,128)(2,1)S(1)}, bf16[24,1024]{1,0:T(8,128)(2,1)S(1)}, u32[]{:S(2)}, u32[]{:S(2)}) collective-permute-start(bf16[24,1024]{1,0:T(8,128)(2,1)S(1)} %collective-permute-done.5), channel_id=1, source_target_pairs={{0,1},{1,2},{2,3},{3,4},{4,5},{5,6},{6,7},{7,0},{8,9},{9,10},{10,1... | collective-permute-start | bytes 147464 | tf_op jit(solution)/shard_map/ppermute | solution.py:12
  41.0 9.7 %collective-permute-start.14 = (bf16[384,128]{1,0:T(8,128)(2,1)S(1)}, bf16[384,128]{1,0:T(8,128)(2,1)S(1)}, u32[]{:S(2)}, u32[]{:S(2)}) collective-permute-start(bf16[384,128]{1,0:T(8,128)(2,1)S(1)} %collective-permute-done.12), channel_id=1, source_target_pairs={{0,32},{32,64},{64,96},{96,128},{128,160},{160,192},{192,224},{224... | collective-permute-start | bytes 294920 | tf_op jit(solution)/shard_map/ppermute | solution.py:83
  42.9 9.7 %collective-permute-start.15 = (bf16[384,128]{1,0:T(8,128)(2,1)S(1)}, bf16[384,128]{1,0:T(8,128)(2,1)S(1)}, u32[]{:S(2)}, u32[]{:S(2)}) collective-permute-start(bf16[384,128]{1,0:T(8,128)(2,1)S(1)} %collective-permute-done.13), channel_id=1, source_target_pairs={{0,480},{32,0},{64,32},{96,64},{128,96},{160,128},{192,160},{224,1... | collective-permute-start | bytes 294920 | tf_op jit(solution)/shard_map/ppermute | solution.py:88
  50.7 7.7 %collective-permute-start.16 = (bf16[384,128]{1,0:T(8,128)(2,1)S(1)}, bf16[384,128]{1,0:T(8,128)(2,1)S(1)}, u32[]{:S(2)}, u32[]{:S(2)}) collective-permute-start(bf16[384,128]{1,0:T(8,128)(2,1)S(1)} %collective-permute-done.14), channel_id=1, source_target_pairs={{0,32},{32,64},{64,96},{96,128},{128,160},{160,192},{192,224},{224... | collective-permute-start | bytes 294920 | tf_op jit(solution)/shard_map/ppermute | solution.py:83
  52.7 7.7 %collective-permute-start.17 = (bf16[384,128]{1,0:T(8,128)(2,1)S(1)}, bf16[384,128]{1,0:T(8,128)(2,1)S(1)}, u32[]{:S(2)}, u32[]{:S(2)}) collective-permute-start(bf16[384,128]{1,0:T(8,128)(2,1)S(1)} %collective-permute-done.15), channel_id=1, source_target_pairs={{0,480},{32,0},{64,32},{96,64},{128,96},{160,128},{192,160},{224,1... | collective-permute-start | bytes 294920 | tf_op jit(solution)/shard_map/ppermute | solution.py:88
  58.4 8.0 %collective-permute-start.18 = (bf16[384,128]{1,0:T(8,128)(2,1)S(1)}, bf16[384,128]{1,0:T(8,128)(2,1)S(1)}, u32[]{:S(2)}, u32[]{:S(2)}) collective-permute-start(bf16[384,128]{1,0:T(8,128)(2,1)S(1)} %collective-permute-done.16), channel_id=1, source_target_pairs={{0,32},{32,64},{64,96},{96,128},{128,160},{160,192},{192,224},{224... | collective-permute-start | bytes 294920 | tf_op jit(solution)/shard_map/ppermute | solution.py:83
  60.4 8.0 %collective-permute-start.19 = (bf16[384,128]{1,0:T(8,128)(2,1)S(1)}, bf16[384,128]{1,0:T(8,128)(2,1)S(1)}, u32[]{:S(2)}, u32[]{:S(2)}) collective-permute-start(bf16[384,128]{1,0:T(8,128)(2,1)S(1)} %collective-permute-done.17), channel_id=1, source_target_pairs={{0,480},{32,0},{64,32},{96,64},{128,96},{160,128},{192,160},{224,1... | collective-permute-start | bytes 294920 | tf_op jit(solution)/shard_map/ppermute | solution.py:88
  66.4 7.8 %collective-permute-start.20 = (bf16[384,128]{1,0:T(8,128)(2,1)S(1)}, bf16[384,128]{1,0:T(8,128)(2,1)S(1)}, u32[]{:S(2)}, u32[]{:S(2)}) collective-permute-start(bf16[384,128]{1,0:T(8,128)(2,1)S(1)} %collective-permute-done.18), channel_id=1, source_target_pairs={{0,32},{32,64},{64,96},{96,128},{128,160},{160,192},{192,224},{224... | collective-permute-start | bytes 294920 | tf_op jit(solution)/shard_map/ppermute | solution.py:83
  68.3 7.8 %collective-permute-start.21 = (bf16[384,128]{1,0:T(8,128)(2,1)S(1)}, bf16[384,128]{1,0:T(8,128)(2,1)S(1)}, u32[]{:S(2)}, u32[]{:S(2)}) collective-permute-start(bf16[384,128]{1,0:T(8,128)(2,1)S(1)} %collective-permute-done.19), channel_id=1, source_target_pairs={{0,480},{32,0},{64,32},{96,64},{128,96},{160,128},{192,160},{224,1... | collective-permute-start | bytes 294920 | tf_op jit(solution)/shard_map/ppermute | solution.py:88
  74.3 8.1 %collective-permute-start.22 = (bf16[384,128]{1,0:T(8,128)(2,1)S(1)}, bf16[384,128]{1,0:T(8,128)(2,1)S(1)}, u32[]{:S(2)}, u32[]{:S(2)}) collective-permute-start(bf16[384,128]{1,0:T(8,128)(2,1)S(1)} %collective-permute-done.20), channel_id=1, source_target_pairs={{0,32},{32,64},{64,96},{96,128},{128,160},{160,192},{192,224},{224... | collective-permute-start | bytes 294920 | tf_op jit(solution)/shard_map/ppermute | solution.py:83
  76.2 8.1 %collective-permute-start.23 = (bf16[384,128]{1,0:T(8,128)(2,1)S(1)}, bf16[384,128]{1,0:T(8,128)(2,1)S(1)}, u32[]{:S(2)}, u32[]{:S(2)}) collective-permute-start(bf16[384,128]{1,0:T(8,128)(2,1)S(1)} %collective-permute-done.21), channel_id=1, source_target_pairs={{0,480},{32,0},{64,32},{96,64},{128,96},{160,128},{192,160},{224,1... | collective-permute-start | bytes 294920 | tf_op jit(solution)/shard_map/ppermute | solution.py:88
  82.4 8.2 %collective-permute-start.24 = (bf16[384,128]{1,0:T(8,128)(2,1)S(1)}, bf16[384,128]{1,0:T(8,128)(2,1)S(1)}, u32[]{:S(2)}, u32[]{:S(2)}) collective-permute-start(bf16[384,128]{1,0:T(8,128)(2,1)S(1)} %collective-permute-done.22), channel_id=1, source_target_pairs={{0,32},{32,64},{64,96},{96,128},{128,160},{160,192},{192,224},{224... | collective-permute-start | bytes 294920 | tf_op jit(solution)/shard_map/ppermute | solution.py:83
  96.0 16.6 %collective-permute-start.25 = (bf16[14,48,128]{2,0,1:T(8,128)(2,1)S(1)}, bf16[14,48,128]{2,0,1:T(8,128)(2,1)S(1)}, u32[]{:S(2)}, u32[]{:S(2)}) collective-permute-start(bf16[14,48,128]{2,0,1:T(8,128)(2,1)S(1)} %get-tuple-element.12), channel_id=1, source_target_pairs={{0,8},{8,16},{16,24},{24,0},{1,9},{9,17},{17,25},{25,1},{2,10},{10... | collective-permute-start | bytes 516104 | tf_op jit(solution)/shard_map/ppermute | solution.py:12
  99.7 24.7 %collective-permute-start.27 = (bf16[14,48,128]{2,0,1:T(8,128)(2,1)}, bf16[14,48,128]{2,0,1:T(8,128)(2,1)}, u32[]{:S(2)}, u32[]{:S(2)}) collective-permute-start(bf16[14,48,128]{2,0,1:T(8,128)(2,1)} %get-tuple-element.13), channel_id=1, source_target_pairs={{0,24},{8,0},{16,8},{24,16},{1,25},{9,1},{17,9},{25,17},{2,26},{10... | collective-permute-start | bytes 516104 | tf_op jit(solution)/shard_map/ppermute | solution.py:12
  108.1 11.1 %copy-start.8 = (bf16[14,4,48,128]{3,0,2,1:T(8,128)(2,1)}, bf16[14,4,48,128]{3,0,2,1:T(8,128)(2,1)S(1)}, u32[]{:S(2)}) copy-start(bf16[14,4,48,128]{3,0,2,1:T(8,128)(2,1)S(1)} %fusion.49) | copy-start | bytes 2064388
  108.9 10.3 %collective-permute-start.7 = (bf16[14,48,128]{2,0,1:T(8,128)(2,1)S(1)}, bf16[14,48,128]{2,0,1:T(8,128)(2,1)S(1)}, u32[]{:S(2)}, u32[]{:S(2)}) collective-permute-start(bf16[14,48,128]{2,0,1:T(8,128)(2,1)S(1)} %get-tuple-element.10), channel_id=1, source_target_pairs={{0,8},{8,16},{16,24},{24,0},{1,9},{9,17},{17,25},{25,1},{2,10},{10... | collective-permute-start | bytes 516104 | tf_op jit(solution)/shard_map/ppermute | solution.py:12
  113.4 11.0 %collective-permute-start.26 = (bf16[14,48,128]{2,0,1:T(8,128)(2,1)}, bf16[14,48,128]{2,0,1:T(8,128)(2,1)}, u32[]{:S(2)}, u32[]{:S(2)}) collective-permute-start(bf16[14,48,128]{2,0,1:T(8,128)(2,1)} %fusion.52), channel_id=1, source_target_pairs={{0,8},{8,16},{16,24},{24,0},{1,9},{9,17},{17,25},{25,1},{2,10},{10... | collective-permute-start | bytes 516104 | tf_op jit(solution)/shard_map/ppermute | solution.py:12
  116.8 8.6 %collective-permute-start.9 = (bf16[14,48,128]{2,0,1:T(8,128)(2,1)}, bf16[14,48,128]{2,0,1:T(8,128)(2,1)}, u32[]{:S(2)}, u32[]{:S(2)}) collective-permute-start(bf16[14,48,128]{2,0,1:T(8,128)(2,1)} %get-tuple-element.11), channel_id=1, source_target_pairs={{0,24},{8,0},{16,8},{24,16},{1,25},{9,1},{17,9},{25,17},{2,26},{10... | collective-permute-start | bytes 516104 | tf_op jit(solution)/shard_map/ppermute | solution.py:12
  120.0 9.2 %collective-permute-start.8 = (bf16[14,48,128]{2,0,1:T(8,128)(2,1)}, bf16[14,48,128]{2,0,1:T(8,128)(2,1)}, u32[]{:S(2)}, u32[]{:S(2)}) collective-permute-start(bf16[14,48,128]{2,0,1:T(8,128)(2,1)} %fusion.58), channel_id=1, source_target_pairs={{0,8},{8,16},{16,24},{24,0},{1,9},{9,17},{17,25},{25,1},{2,10},{10... | collective-permute-start | bytes 516104 | tf_op jit(solution)/shard_map/ppermute | solution.py:12
  131.5 13.8 %collective-permute-start.29 = (bf16[14,48,128]{2,0,1:T(8,128)(2,1)}, bf16[14,48,128]{2,0,1:T(8,128)(2,1)S(1)}, u32[]{:S(2)}, u32[]{:S(2)}) collective-permute-start(bf16[14,48,128]{2,0,1:T(8,128)(2,1)} %get-tuple-element.8), channel_id=1, source_target_pairs={{0,8},{8,16},{16,24},{24,0},{1,9},{9,17},{17,25},{25,1},{2,10},{10... | collective-permute-start | bytes 516104 | tf_op jit(solution)/shard_map/ppermute | solution.py:12
  134.0 13.3 %collective-permute-start.32 = (bf16[14,48,128]{2,0,1:T(8,128)(2,1)}, bf16[14,48,128]{2,0,1:T(8,128)(2,1)S(1)}, u32[]{:S(2)}, u32[]{:S(2)}) collective-permute-start(bf16[14,48,128]{2,0,1:T(8,128)(2,1)} %get-tuple-element.9), channel_id=1, source_target_pairs={{0,8},{8,16},{16,24},{24,0},{1,9},{9,17},{17,25},{25,1},{2,10},{10... | collective-permute-start | bytes 516104 | tf_op jit(solution)/shard_map/ppermute | solution.py:12
  137.7 13.0 %collective-permute-start.28 = (bf16[14,48,128]{2,0,1:T(8,128)(2,1)}, bf16[14,48,128]{2,0,1:T(8,128)(2,1)}, u32[]{:S(2)}, u32[]{:S(2)}) collective-permute-start(bf16[14,48,128]{2,0,1:T(8,128)(2,1)} %get-tuple-element.8), channel_id=1, source_target_pairs={{0,24},{8,0},{16,8},{24,16},{1,25},{9,1},{17,9},{25,17},{2,26},{10... | collective-permute-start | bytes 516104 | tf_op jit(solution)/shard_map/ppermute | solution.py:12
  140.2 10.4 %collective-permute-start.31 = (bf16[14,48,128]{2,0,1:T(8,128)(2,1)}, bf16[14,48,128]{2,0,1:T(8,128)(2,1)S(1)}, u32[]{:S(2)}, u32[]{:S(2)}) collective-permute-start(bf16[14,48,128]{2,0,1:T(8,128)(2,1)} %get-tuple-element.9), channel_id=1, source_target_pairs={{0,24},{8,0},{16,8},{24,16},{1,25},{9,1},{17,9},{25,17},{2,26},{10... | collective-permute-start | bytes 516104 | tf_op jit(solution)/shard_map/ppermute | solution.py:12
  145.4 8.6 %collective-permute-start.30 = (bf16[14,48,128]{2,0,1:T(8,128)(2,1)S(1)}, bf16[14,48,128]{2,0,1:T(8,128)(2,1)S(1)}, u32[]{:S(2)}, u32[]{:S(2)}) collective-permute-start(bf16[14,48,128]{2,0,1:T(8,128)(2,1)S(1)} %collective-permute-done.29), channel_id=1, source_target_pairs={{0,8},{8,16},{16,24},{24,0},{1,9},{9,17},{17,25},{25,1},{2,10},{10... | collective-permute-start | bytes 516104 | tf_op jit(solution)/shard_map/ppermute | solution.py:12
  147.3 8.8 %collective-permute-start.33 = (bf16[14,48,128]{2,0,1:T(8,128)(2,1)S(1)}, bf16[14,48,128]{2,0,1:T(8,128)(2,1)S(1)}, u32[]{:S(2)}, u32[]{:S(2)}) collective-permute-start(bf16[14,48,128]{2,0,1:T(8,128)(2,1)S(1)} %collective-permute-done.32), channel_id=1, source_target_pairs={{0,8},{8,16},{16,24},{24,0},{1,9},{9,17},{17,25},{25,1},{2,10},{10... | collective-permute-start | bytes 516104 | tf_op jit(solution)/shard_map/ppermute | solution.py:12
  150.7 5.4 %copy-start.10 = (bf16[14,48,128]{2,0,1:T(8,128)(2,1)}, bf16[14,48,128]{2,0,1:T(8,128)(2,1)S(1)}, u32[]{:S(2)}) copy-start(bf16[14,48,128]{2,0,1:T(8,128)(2,1)S(1)} %collective-permute-done.31) | copy-start | bytes 516100
  165.0 148.9 %reduce-scatter.3.cloned.1.call-start = ((), (), s32[]{:S(2)}) async-start(), calls=%async_computation.3 | async-start | bytes 1671168 | tf_op jit(solution)/shard_map/reduce_scatter | solution.py:144
  177.6 3.5 %collective-permute-start.34 = (bf16[8,24,128]{2,0,1:T(8,128)(2,1)S(1)}, bf16[8,24,128]{2,0,1:T(8,128)(2,1)S(1)}, u32[]{:S(2)}, u32[]{:S(2)}) collective-permute-start(bf16[8,24,128]{2,0,1:T(8,128)(2,1)S(1)} %get-tuple-element.16), channel_id=1, source_target_pairs={{0,1},{1,2},{2,3},{3,4},{4,5},{5,6},{6,7},{7,0},{8,9},{9,10},{10,1... | collective-permute-start | bytes 147464 | tf_op jit(solution)/shard_map/ppermute | solution.py:12
  181.2 3.5 %collective-permute-start.35 = (bf16[8,24,128]{2,0,1:T(8,128)(2,1)S(1)}, bf16[8,24,128]{2,0,1:T(8,128)(2,1)S(1)}, u32[]{:S(2)}, u32[]{:S(2)}) collective-permute-start(bf16[8,24,128]{2,0,1:T(8,128)(2,1)S(1)} %fusion.67), channel_id=1, source_target_pairs={{0,1},{1,2},{2,3},{3,4},{4,5},{5,6},{6,7},{7,0},{8,9},{9,10},{10,1... | collective-permute-start | bytes 147464 | tf_op jit(solution)/shard_map/ppermute | solution.py:12
  183.7 4.8 %collective-permute-start.38 = (bf16[8,24,128]{2,0,1:T(8,128)(2,1)S(1)}, bf16[8,24,128]{2,0,1:T(8,128)(2,1)S(1)}, u32[]{:S(2)}, u32[]{:S(2)}) collective-permute-start(bf16[8,24,128]{2,0,1:T(8,128)(2,1)S(1)} %get-tuple-element.17), channel_id=1, source_target_pairs={{0,7},{1,0},{2,1},{3,2},{4,3},{5,4},{6,5},{7,6},{8,15},{9,8},{10,9... | collective-permute-start | bytes 147464 | tf_op jit(solution)/shard_map/ppermute | solution.py:12
  184.7 4.7 %collective-permute-start.36 = (bf16[8,24,128]{2,0,1:T(8,128)(2,1)S(1)}, bf16[8,24,128]{2,0,1:T(8,128)(2,1)S(1)}, u32[]{:S(2)}, u32[]{:S(2)}) collective-permute-start(bf16[8,24,128]{2,0,1:T(8,128)(2,1)S(1)} %fusion.66), channel_id=1, source_target_pairs={{0,1},{1,2},{2,3},{3,4},{4,5},{5,6},{6,7},{7,0},{8,9},{9,10},{10,1... | collective-permute-start | bytes 147464 | tf_op jit(solution)/shard_map/ppermute | solution.py:12
  189.4 4.6 %collective-permute-start.39 = (bf16[8,24,128]{2,0,1:T(8,128)(2,1)S(1)}, bf16[8,24,128]{2,0,1:T(8,128)(2,1)S(1)}, u32[]{:S(2)}, u32[]{:S(2)}) collective-permute-start(bf16[8,24,128]{2,0,1:T(8,128)(2,1)S(1)} %get-tuple-element.15), channel_id=1, source_target_pairs={{0,7},{1,0},{2,1},{3,2},{4,3},{5,4},{6,5},{7,6},{8,15},{9,8},{10,9... | collective-permute-start | bytes 147464 | tf_op jit(solution)/shard_map/ppermute | solution.py:12
  189.4 4.7 %collective-permute-start.37 = (bf16[8,24,128]{2,0,1:T(8,128)(2,1)S(1)}, bf16[8,24,128]{2,0,1:T(8,128)(2,1)S(1)}, u32[]{:S(2)}, u32[]{:S(2)}) collective-permute-start(bf16[8,24,128]{2,0,1:T(8,128)(2,1)S(1)} %get-tuple-element.14), channel_id=1, source_target_pairs={{0,1},{1,2},{2,3},{3,4},{4,5},{5,6},{6,7},{7,0},{8,9},{9,10},{10,1... | collective-permute-start | bytes 147464 | tf_op jit(solution)/shard_map/ppermute | solution.py:12
  194.0 5.3 %collective-permute-start.40 = (bf16[8,24,128]{2,0,1:T(8,128)(2,1)S(1)}, bf16[8,24,128]{2,0,1:T(8,128)(2,1)S(1)}, u32[]{:S(2)}, u32[]{:S(2)}) collective-permute-start(bf16[8,24,128]{2,0,1:T(8,128)(2,1)S(1)} %fusion.61), channel_id=1, source_target_pairs={{0,7},{1,0},{2,1},{3,2},{4,3},{5,4},{6,5},{7,6},{8,15},{9,8},{10,9... | collective-permute-start | bytes 147464 | tf_op jit(solution)/shard_map/ppermute | solution.py:12
  (10 other events, 20.8 us)
Sparse Core Ops, SparseCore 0:
  21.2 71.5 all-gather.1
  165.1 75.3 reduce-scatter.4
  243.4 70.4 reduce-scatter.2
